TPU v7x, 256 devices: a whole 4x4x8 slice. The times are simulated.
256 devices in a mesh: row: 16 (over x_hi, y, core), col: 16 (over z, x_lo).
Axes of the slice: x: 4 (x_hi: 2, x_lo: 2; x = x_hi * 2 + x_lo), y: 4, z: 8, core: 2. Of those that a mesh axis runs over, the one named last changes fastest.
Arguments:
- stem: bfloat16 [16, 16, 1, 512, 2, 512], P('row', 'col'), may hold values from -6 to 6
- branch: bfloat16 [16, 4, 2, 512, 512], P('row', None, None, None, 'col'), may hold values from -0.1875 to 0.1875
Outputs:
- amplitudes: bfloat16 [16, 16, 1, 512, 2, 512], P('row', 'col')
All inputs are finite; a program needn't handle non-finite values.
Results may differ from a plain program's by a relative error of at most 0.0075.
Values may be sent and summed in bfloat16 or wider, within the bound.
No kernel may reach another device: no remote copies, remote signals or barrier semaphores. Data moves between devices by JAX's collectives and lax.ppermute only.
A program may use at most 64 MiB of HBM per device.

v0:
```python
import jax
import jax.numpy as jnp
from jax import lax
from jax.sharding import PartitionSpec as P


def right_piece(block, piece):
    width = piece.shape[2]
    items = block.shape[0]
    order_size = block.shape[1]
    flat = block.reshape(items * order_size, 2 * width)
    real_t = piece[0].T
    imag_t = piece[1].T
    weight = jnp.block([[real_t, imag_t], [-imag_t, real_t]])
    product = jnp.dot(flat, weight, preferred_element_type=jnp.float32)
    return product.reshape(items, order_size, 2, order_size)


def left_piece(block, piece):
    rows_out = piece.shape[1]
    real_in = block[:, :, 0, :]
    imag_in = block[:, :, 1, :]
    real_w = piece[0]
    imag_w = piece[1]
    weight_real = jnp.concatenate([real_w, imag_w], axis=0)
    weight_imag = jnp.concatenate([-imag_w, real_w], axis=0)
    product = jnp.einsum("xi,eij->exj", weight_real, real_in, preferred_element_type=jnp.float32)
    product = product + jnp.einsum(
        "xi,eij->exj", weight_imag, imag_in, preferred_element_type=jnp.float32
    )
    return jnp.stack([product[:, :rows_out, :], product[:, rows_out:, :]], axis=2)


def shards(stem, branch):
    slab_count = stem.shape[2]
    order_size = stem.shape[3]
    row_count = lax.axis_size("row")
    share = order_size // row_count
    own_columns = branch[0]
    whole = lax.all_gather(own_columns, "col", axis=3, tiled=True)

    def apply_right(block, build_id):
        return right_piece(block, whole[build_id])

    def apply_left(block, build_id):
        return left_piece(block, whole[build_id])

    block = stem[0, 0]
    half_first = apply_right(block, 1).astype(jnp.bfloat16)
    step_first = apply_left(half_first, 0).astype(jnp.bfloat16)
    outgoing = step_first.reshape(slab_count, row_count, share, 2, order_size)
    moved = lax.all_to_all(outgoing, "row", split_axis=1, concat_axis=1, tiled=True)
    items = moved.shape[0]
    flat = moved.reshape(items, order_size, 2, order_size)
    half_second = apply_right(flat, 3).astype(jnp.bfloat16)
    step_second = apply_left(half_second, 2).astype(jnp.bfloat16)
    leaving = step_second.reshape(slab_count, order_size, 2, row_count, share)
    arrived = lax.all_to_all(leaving, "row", split_axis=3, concat_axis=3, tiled=True)
    return arrived.reshape(1, 1, slab_count, order_size, 2, order_size)


def solution(mesh):
    placed = (P("row", "col", None, None, None, None), P("row", None, None, None, "col"))
    return jax.shard_map(
        shards,
        mesh=mesh,
        in_specs=placed,
        out_specs=P("row", "col", None, None, None, None),
        check_vma=False,
    )
```

profile of v0, /device:TPU:1, one launch (start us, length us, event | category | flops | bytes accessed | tf_op | source)
XLA Modules:
  0.0 182.5 jit_solution(8665607085128221393)
XLA Ops:
  6.5 0.0 all-gather.3.cloned.1.call-start
  6.5 0.7 all-gather.3.cloned.1.call-update
  7.3 1.5 copy.20
  8.7 100.9 %all-gather.3.cloned.1.call-done = bf16[1,4,2,512,512]{3,4,2,1,0:T(8,128)(2,1)} async-done(((bf16[1,4,2,512,32]{3,4,2,1,0:T(8,128)(2,1)}), bf16[1,4,2,512,512]{3,4,2,1,0:T(8,128)(2,1)}) %all-gather.3.cloned.1.call-update) | async-done | bytes 4194320 | tf_op jit(solution)/shard_map/all_gather | solution.py:40
  109.6 2.2 %fusion.36 = (bf16[512,512]{0,1:T(8,128)(2,1)}, bf16[512,512]{0,1:T(8,128)(2,1)S(1)}) fusion(bf16[4,2,512,512]{2,3,1,0:T(8,128)(2,1)} %bitcast.76), kind=kLoop, calls=%fused_computation.52 | loop fusion | flops 524288 | bytes 2097152 | tf_op jit(solution)/shard_map/neg | solution.py:26
  111.8 2.1 %fusion.35 = (bf16[512,512]{1,0:T(8,128)(2,1)}, bf16[512,512]{1,0:T(8,128)(2,1)S(1)}) fusion(bf16[4,2,512,512]{2,3,1,0:T(8,128)(2,1)} %bitcast.77), kind=kLoop, calls=%fused_computation.51 | loop fusion | flops 524288 | bytes 2097152 | tf_op jit(solution)/shard_map/neg | solution.py:14
  113.9 0.0 copy-done
  113.9 1.5 slice_bitcast_fusion.6
  115.4 1.3 fusion.8
  116.7 0.7 fusion.14
  117.4 0.7 fusion.12
  118.1 0.1 fusion.38
  118.2 0.2 copy.11
  118.4 0.2 copy.12
  118.7 0.1 pad_maximum_fusion
  118.8 1.0 copy.13
  119.8 9.4 %all-to-all-start = ((bf16[1,16,32,2,512]{4,2,3,0,1:T(8,128)(2,1)}), bf16[1,16,32,2,512]{4,2,3,0,1:T(8,128)(2,1)S(1)}, u32[]{:S(2)}, u32[]{:S(2)}) async-start(bf16[1,16,32,2,512]{4,2,3,0,1:T(8,128)(2,1)} %copy.13), calls=%async_computation | async-start | bytes 2097152 | tf_op jit(solution)/shard_map/all_to_all | solution.py:52
  129.2 1.8 maximum_bitcast_fusion
  131.0 2.6 %copy.15 = bf16[1024,1024]{1,0:T(8,128)(2,1)} copy(bf16[1024,1024]{0,1:T(8,128)(2,1)S(1)} %maximum_bitcast_fusion) | data formatting | bytes 4194304 | tf_op jit(solution)/shard_map/dot_general | solution.py:15
  133.6 12.7 %all-to-all-done = bf16[1,16,32,2,512]{4,2,3,0,1:T(8,128)(2,1)S(1)} async-done(((bf16[1,16,32,2,512]{4,2,3,0,1:T(8,128)(2,1)}), bf16[1,16,32,2,512]{4,2,3,0,1:T(8,128)(2,1)S(1)}, u32[]{:S(2)}, u32[]{:S(2)}) %all-to-all-start) | async-done | bytes 1048608 | tf_op jit(solution)/shard_map/all_to_all | solution.py:52
  146.3 1.1 copy.14
  147.3 0.8 reshape.153
  148.1 0.0 copy-start.1
  148.1 3.0 %fusion.11 = bf16[1,512,2,512]{3,1,2,0:T(8,128)(2,1)S(1)} fusion(bf16[512,1024,1]{1,0,2:T(8,128)(2,1)S(1)} %reshape.153, bf16[2,512,1024]{2,1,0:T(8,128)(2,1)} %bitcast.80), kind=kOutput, calls=%fused_computation.13 | convolution fusion | flops 1074266112 | bytes 4194304 | tf_op jit(solution)/shard_map/dot_general | solution.py:15
  151.1 0.7 fusion.21
  151.9 0.3 copy-done.2
  152.2 0.7 fusion.13
  152.9 0.1 fusion.37
  153.0 0.1 pad_maximum_fusion.1
  153.1 20.3 %all_to_all.10 = bf16[1,512,2,16,32]{1,4,2,0,3:T(8,128)(2,1)S(1)} all-to-all(bf16[1,512,2,16,32]{1,4,2,0,3:T(8,128)(2,1)S(1)} %pad_maximum_fusion.1), channel_id=1, replica_groups=mesh['row'=16,'col'=16] {'row'}, dimensions={3} | all-to-all | bytes 2097152 | tf_op jit(solution)/shard_map/all_to_all | solution.py:58
  173.4 0.1 copy.18
  173.5 2.1 %copy.19 = bf16[1,1,1,512,2,512]{5,4,3,2,1,0:T(2,128)(2,1)} copy(bf16[1,1,1,512,2,512]{3,5,4,2,1,0:T(8,128)(2,1)S(1)} %bitcast.79) | data formatting | bytes 2097152 | tf_op jit(solution)/shard_map/reshape | solution.py:59
  (5 shorter events, 0.0 us)
Async XLA Ops:
  6.5 103.1 %all-gather.3.cloned.1.call-start = ((), (), s32[]{:S(2)}) async-start(), calls=%async_computation.2 | async-start | bytes 4456448 | tf_op jit(solution)/shard_map/all_gather | solution.py:40
  109.6 4.3 %copy-start = (bf16[1,4,2,512,512]{3,4,2,1,0:T(8,128)(2,1)S(1)}, bf16[1,4,2,512,512]{3,4,2,1,0:T(8,128)(2,1)}, u32[]{:S(2)}) copy-start(bf16[1,4,2,512,512]{3,4,2,1,0:T(8,128)(2,1)} %all-gather.3.cloned.1.call-done) | copy-start | bytes 12582916
  119.8 26.4 %all-to-all-start = ((bf16[1,16,32,2,512]{4,2,3,0,1:T(8,128)(2,1)}), bf16[1,16,32,2,512]{4,2,3,0,1:T(8,128)(2,1)S(1)}, u32[]{:S(2)}, u32[]{:S(2)}) async-start(bf16[1,16,32,2,512]{4,2,3,0,1:T(8,128)(2,1)} %copy.13), calls=%async_computation | async-start | bytes 2097152 | tf_op jit(solution)/shard_map/all_to_all | solution.py:52
  148.1 3.0 %copy-start.1 = (bf16[512,512]{0,1:T(8,128)(2,1)S(1)}, bf16[512,512]{0,1:T(8,128)(2,1)}, u32[]{:S(2)}) copy-start(bf16[512,512]{0,1:T(8,128)(2,1)} %get-tuple-element.9) | copy-start | bytes 1572868
  148.1 3.0 %copy-start.3 = (bf16[512,512]{0,1:T(8,128)(2,1)S(1)}, bf16[512,512]{0,1:T(8,128)(2,1)}, u32[]{:S(2)}) copy-start(bf16[512,512]{0,1:T(8,128)(2,1)} %get-tuple-element.8) | copy-start | bytes 1572868
  151.1 1.0 copy-start.2
Sparse Core Ops, SparseCore 0:
  9.1 100.4 all-gather.2
where the time goes:
time: 183 us; the launch traced here: 182 us
  waiting for transfers between devices  114 us (62%)
  blocking collectives  20.3 us (11%)
  between operations  13.5 us (7%)
  local copies, waits for them, and re-layouts  11.6 us (6%)
  starting transfers between devices  9.37 us (5%)
  matrix products  7.15 us (4%)
  other arithmetic  6.25 us (3%)
    all_gather x1, waiting for transfers between devices, shards(): whole = lax.all_gather(own_columns, 'col', axis=3, tiled=True)  101 us
    all_to_all x1, blocking collectives, shards(): lax.all_to_all(leaving, 'row', split_axis=3, concat_axis=3, tiled=True)  20.3 us
    all_to_all x1, waiting for transfers between devices, shards(): lax.all_to_all(outgoing, 'row', split_axis=1, concat_axis=1, tiled=True)  12.7 us
    all_to_all x1, starting transfers between devices, shards(): lax.all_to_all(outgoing, 'row', split_axis=1, concat_axis=1, tiled=True)  9.37 us
    dot_general x2, matrix products, right_piece(): product = jnp.dot(flat, weight, preferred_element_type=jnp.float32)  4.26 us
  transfers between devices with their start and end apart: 2, of which 2 were waited for; matrix products, arithmetic and copies ran while one was open for 3% of the time, Pallas kernels for 0%

commit v1 on v0

--- a/solution.py
+++ b/solution.py
@@ -37,7 +37,9 @@
     row_count = lax.axis_size("row")
     share = order_size // row_count
     own_columns = branch[0]
-    whole = lax.all_gather(own_columns, "col", axis=3, tiled=True)
+    whole = jnp.concatenate(
+        lax.all_to_all(jnp.stack([own_columns] * lax.axis_size("col")), "col", 0, 0), axis=3
+    )
 
     def apply_right(block, build_id):
         return right_piece(block, whole[build_id])

time: 183 us -> 177 us (0.967)
  between operations: 13.5 us -> 0.17 us
  starting transfers between devices: 9.37 us -> 18.3 us
  local copies, waits for them, and re-layouts: 11.6 us -> 17.4 us
  waiting for transfers between devices: 114 us -> 110 us
  other arithmetic: 6.25 us -> 3.74 us
    all_gather x1 -> x0, waiting for transfers between devices: 101 us -> none  [shards(): whole = lax.all_gather(own_columns, 'col', axis=3, tiled=True)]
    all_to_all x0 -> x1, waiting for transfers between devices: none -> 96.7 us  [shards(): lax.all_to_all(jnp.stack([own_columns] * lax.axis_size('col')), 'col', 0, 0)]
    all_to_all x0 -> x1, starting transfers between devices: none -> 10.2 us  [shards(): lax.all_to_all(jnp.stack([own_columns] * lax.axis_size('col')), 'col', 0, 0)]
    another operation x0 -> x1, local copies, waits for them, and re-layouts: none -> 3.43 us  [shards(): jnp.stack([own_columns] * lax.axis_size('col'))]
    all_to_all x0 -> x1, local copies, waits for them, and re-layouts: none -> 2.66 us  [shards(): lax.all_to_all(jnp.stack([own_columns] * lax.axis_size('col')), 'col', 0, 0)]
where the time goes in v1:
time: 177 us
  waiting for transfers between devices  110 us (62%)
  blocking collectives  20.3 us (11%)
  starting transfers between devices  18.3 us (10%)
  local copies, waits for them, and re-layouts  17.4 us (10%)
  matrix products  7.12 us (4%)
  other arithmetic  3.74 us (2%)
    all_to_all x1, waiting for transfers between devices, shards(): lax.all_to_all(jnp.stack([own_columns] * lax.axis_size('col')), 'col', 0, 0)  96.7 us
    all_to_all x1, blocking collectives, shards(): lax.all_to_all(leaving, 'row', split_axis=3, concat_axis=3, tiled=True)  20.3 us
    all_to_all x1, waiting for transfers between devices, shards(): lax.all_to_all(outgoing, 'row', split_axis=1, concat_axis=1, tiled=True)  13 us
    all_to_all x1, starting transfers between devices, shards(): lax.all_to_all(jnp.stack([own_columns] * lax.axis_size('col')), 'col', 0, 0)  10.2 us
    all_to_all x1, starting transfers between devices, shards(): lax.all_to_all(outgoing, 'row', split_axis=1, concat_axis=1, tiled=True)  8.1 us
    dot_general x2, matrix products, right_piece(): product = jnp.dot(flat, weight, preferred_element_type=jnp.float32)  4.22 us
  transfers between devices with their start and end apart: 2, of which 2 were waited for; matrix products, arithmetic and copies ran while one was open for 3% of the time, Pallas kernels for 0%

profile of v1, /device:TPU:1, one launch (start us, length us, event | category | flops | bytes accessed | tf_op | source)
XLA Modules:
  0.0 176.8 jit_solution(9720128637591819598)
XLA Ops:
  0.0 3.4 %stack.21 = bf16[16,4,2,512,32]{3,4,2,1,0:T(8,128)(2,1)} broadcast(bf16[4,2,512,32]{2,3,1,0:T(8,128)(2,1)} %bitcast.88), dimensions={1,2,3,4} | broadcast | bytes 4456448 | tf_op jit(solution)/shard_map/stack | solution.py:41
  3.4 10.2 %all-to-all-start = ((bf16[16,4,2,512,32]{3,4,2,1,0:T(8,128)(2,1)}), bf16[16,4,2,512,32]{3,4,2,1,0:T(8,128)(2,1)}, u32[]{:S(2)}, u32[]{:S(2)}) async-start(bf16[16,4,2,512,32]{3,4,2,1,0:T(8,128)(2,1)} %stack.21), calls=%async_computation | async-start | bytes 8388608 | tf_op jit(solution)/shard_map/all_to_all | solution.py:41
  13.7 0.0 copy-done.3
  13.7 0.2 copy.21
  13.9 96.7 %all-to-all-done = bf16[16,4,2,512,32]{3,4,2,1,0:T(8,128)(2,1)} async-done(((bf16[16,4,2,512,32]{3,4,2,1,0:T(8,128)(2,1)}), bf16[16,4,2,512,32]{3,4,2,1,0:T(8,128)(2,1)}, u32[]{:S(2)}, u32[]{:S(2)}) %all-to-all-start) | async-done | bytes 4194336 | tf_op jit(solution)/shard_map/all_to_all | solution.py:41
  110.6 2.7 %copy.23 = bf16[16,4,2,512,32]{3,4,0,2,1:T(8,128)(2,1)S(1)} copy(bf16[16,4,2,512,32]{3,4,2,1,0:T(8,128)(2,1)} %all-to-all-done) | data formatting | bytes 8388608 | tf_op jit(solution)/shard_map/all_to_all | solution.py:41
  113.3 1.3 fusion.33
  114.6 1.0 bitcast_negate_fusion.1
  115.6 0.9 bitcast_negate_fusion
  116.5 1.3 fusion.8
  117.8 0.7 fusion.14
  118.5 0.7 fusion.12
  119.2 0.1 fusion.35
  119.3 0.2 copy.12
  119.5 0.2 copy.13
  119.8 0.1 pad_maximum_fusion
  119.9 1.0 copy.14
  120.9 8.1 %all-to-all-start.1 = ((bf16[1,16,32,2,512]{4,2,3,0,1:T(8,128)(2,1)}), bf16[1,16,32,2,512]{4,2,3,0,1:T(8,128)(2,1)}, u32[]{:S(2)}, u32[]{:S(2)}) async-start(bf16[1,16,32,2,512]{4,2,3,0,1:T(8,128)(2,1)} %copy.14), calls=%async_computation.1 | async-start | bytes 2097152 | tf_op jit(solution)/shard_map/all_to_all | solution.py:54
  129.0 1.6 maximum_bitcast_fusion
  130.6 2.6 %copy.16 = bf16[1024,1024]{1,0:T(8,128)(2,1)} copy(bf16[1024,1024]{0,1:T(8,128)(2,1)S(1)} %maximum_bitcast_fusion) | data formatting | bytes 4194304 | tf_op jit(solution)/shard_map/dot_general | solution.py:15
  133.2 13.0 %all-to-all-done.1 = bf16[1,16,32,2,512]{4,2,3,0,1:T(8,128)(2,1)} async-done(((bf16[1,16,32,2,512]{4,2,3,0,1:T(8,128)(2,1)}), bf16[1,16,32,2,512]{4,2,3,0,1:T(8,128)(2,1)}, u32[]{:S(2)}, u32[]{:S(2)}) %all-to-all-start.1) | async-done | bytes 1048608 | tf_op jit(solution)/shard_map/all_to_all | solution.py:54
  146.2 2.3 %copy.15 = bf16[1,16,32,2,512]{4,3,2,1,0:T(2,128)(2,1)S(1)} copy(bf16[1,16,32,2,512]{4,2,3,0,1:T(8,128)(2,1)} %all-to-all-done.1) | data formatting | bytes 2097152 | tf_op jit(solution)/shard_map/all_to_all | solution.py:54
  148.5 0.8 reshape.166
  149.3 2.9 %fusion.11 = bf16[1,512,2,512]{3,1,2,0:T(8,128)(2,1)S(1)} fusion(bf16[512,1024,1]{1,0,2:T(8,128)(2,1)S(1)} %reshape.166, bf16[2,512,1024]{2,1,0:T(8,128)(2,1)} %bitcast.76), kind=kOutput, calls=%fused_computation.14 | convolution fusion | flops 1074266112 | bytes 4194304 | tf_op jit(solution)/shard_map/dot_general | solution.py:15
  152.2 0.7 fusion.21
  153.0 0.3 copy-done.2
  153.3 0.7 fusion.13
  154.0 0.1 fusion.34
  154.1 0.1 pad_maximum_fusion.1
  154.2 20.3 %all_to_all.15 = bf16[1,512,2,16,32]{1,4,2,0,3:T(8,128)(2,1)S(1)} all-to-all(bf16[1,512,2,16,32]{1,4,2,0,3:T(8,128)(2,1)S(1)} %pad_maximum_fusion.1), channel_id=1, replica_groups=mesh['row'=16,'col'=16] {'row'}, dimensions={3} | all-to-all | bytes 2097152 | tf_op jit(solution)/shard_map/all_to_all | solution.py:60
  174.5 0.1 copy.19
  174.7 2.1 %copy.20 = bf16[1,1,1,512,2,512]{5,4,3,2,1,0:T(2,128)(2,1)} copy(bf16[1,1,1,512,2,512]{3,5,4,2,1,0:T(8,128)(2,1)S(1)} %bitcast.72) | data formatting | bytes 2097152 | tf_op jit(solution)/shard_map/reshape | solution.py:61
  (6 shorter events, 0.0 us)
Async XLA Ops:
  3.4 10.2 %copy-start.3 = (bf16[1,1,1,512,2,512]{5,4,3,2,1,0:T(2,128)(2,1)S(1)}, bf16[1,1,1,512,2,512]{5,4,3,2,1,0:T(2,128)(2,1)}, u32[]{:S(2)}) copy-start(bf16[1,1,1,512,2,512]{5,4,3,2,1,0:T(2,128)(2,1)} %param.2) | copy-start | bytes 3145732
  3.4 107.2 %all-to-all-start = ((bf16[16,4,2,512,32]{3,4,2,1,0:T(8,128)(2,1)}), bf16[16,4,2,512,32]{3,4,2,1,0:T(8,128)(2,1)}, u32[]{:S(2)}, u32[]{:S(2)}) async-start(bf16[16,4,2,512,32]{3,4,2,1,0:T(8,128)(2,1)} %stack.21), calls=%async_computation | async-start | bytes 8388608 | tf_op jit(solution)/shard_map/all_to_all | solution.py:41
  114.6 1.9 %copy-start = (bf16[1,1,512,16,32]{2,4,3,1,0:T(8,128)(2,1)}, bf16[1,1,512,16,32]{2,4,3,1,0:T(8,128)(2,1)S(1)}, u32[]{:S(2)}) copy-start(bf16[1,1,512,16,32]{2,4,3,1,0:T(8,128)(2,1)S(1)} %get-tuple-element.6) | copy-start | bytes 1572868
  120.9 25.3 %all-to-all-start.1 = ((bf16[1,16,32,2,512]{4,2,3,0,1:T(8,128)(2,1)}), bf16[1,16,32,2,512]{4,2,3,0,1:T(8,128)(2,1)}, u32[]{:S(2)}, u32[]{:S(2)}) async-start(bf16[1,16,32,2,512]{4,2,3,0,1:T(8,128)(2,1)} %copy.14), calls=%async_computation.1 | async-start | bytes 2097152 | tf_op jit(solution)/shard_map/all_to_all | solution.py:54
  149.3 2.9 %copy-start.1 = (bf16[1,1,512,16,32]{2,4,3,1,0:T(8,128)(2,1)S(1)}, bf16[1,1,512,16,32]{2,4,3,1,0:T(8,128)(2,1)}, u32[]{:S(2)}) copy-start(bf16[1,1,512,16,32]{2,4,3,1,0:T(8,128)(2,1)} %copy-done) | copy-start | bytes 1572868
  152.2 1.0 copy-start.2
